TPU v7x, 768 devices: a whole 4x8x12 slice. The times are simulated.
768 devices in a mesh: rep: 12 (over z), fsdp: 64 (over y, x, core).
Axes of the slice: x: 4, y: 8, z: 12, core: 2. Of those that a mesh axis runs over, the one named last changes fastest.
Arguments:
- acts: bfloat16 [12, 32768, 3072], P('rep', 'fsdp'), may hold values from -16 to 16
- cotangent: bfloat16 [12, 32768, 512], P('rep', 'fsdp'), may hold values from -0.03125 to 0.03125
- nonfinite_row_mask: int32 [12, 3072], P('rep', 'fsdp'), may hold values from 0 to 1, as said below
- params: float32 [12, 3072, 512], P('rep', 'fsdp'), may hold values from -6 to 6
- adam_first_state: float32 [12, 3072, 512], P('rep', 'fsdp'), may hold values from -6 to 6
- adam_second_state: float32 [12, 3072, 512], P('rep', 'fsdp'), may hold values from 0.2 to 4
- anchor: float32 [3072, 512], P('fsdp'), may hold values from -6 to 6
- momentum: float32 [3072, 512], P('fsdp'), may hold values from -3 to 3
Outputs:
- anchor_next: float32 [3072, 512], P('fsdp')
- momentum_next: float32 [3072, 512], P('fsdp')
- first_next: float32 [12, 3072, 512], P('rep', 'fsdp')
- second_next: float32 [12, 3072, 512], P('rep', 'fsdp')
Inputs may be any that keep to these rules, and one draw needn't show every extreme that they name: `nonfinite_row_mask`: exactly one replica has a marked row, and it has exactly one; all other replicas have none.
All inputs are finite; a program needn't handle non-finite values.
Results may differ from a plain program's by a relative error of at most 0.0003.
Values may be sent and summed in bfloat16 or wider, within the bound.
No kernel may reach another device: no remote copies, remote signals or barrier semaphores. Data moves between devices by JAX's collectives and lax.ppermute only.
A program may use at most 128 MiB of HBM per device.

v0:
```python
import jax
import jax.numpy as jnp
from jax import lax
from jax.sharding import PartitionSpec as P

corr_first = 1.0 - 0.9**10
corr_second = 1.0 - 0.95**10


def body(
    acts,
    cotangent,
    nonfinite_row_mask,
    params,
    adam_first_state,
    adam_second_state,
    anchor,
    momentum,
):
    inputs = acts[0]
    upstream = cotangent[0]
    contract = (((0,), (0,)), ((), ()))
    gradient_value = lax.psum_scatter(
        lax.dot_general(inputs, upstream, contract, preferred_element_type=jnp.float32),
        "fsdp",
        scatter_dimension=0,
        tiled=True,
    )
    corrupted_gradient = jnp.where(
        (nonfinite_row_mask[0] == 1)[:, None], jnp.float32(jnp.nan), gradient_value
    )
    replica_nonfinite = jnp.any(jnp.isnan(corrupted_gradient)).astype(jnp.int32)
    first_state_value = 0.9 * adam_first_state[0] + 0.1 * corrupted_gradient
    second_state_value = (
        0.95 * adam_second_state[0] + 0.05 * corrupted_gradient * corrupted_gradient
    )
    update = first_state_value / corr_first / (jnp.sqrt(second_state_value / corr_second) + 1e-08)
    inner = params[0] - 0.1 * (update + 0.1 * params[0])
    pseudo = anchor - inner
    replica_bad = lax.pmax(replica_nonfinite, "fsdp")
    keep = replica_bad == 0
    share = jnp.where(keep, pseudo, jnp.float32(0.0))
    total, count = lax.psum((share, keep.astype(jnp.float32)), "rep")
    average = total / count
    momentum_next = 0.9 * momentum + average
    anchor_next = anchor - 0.7 * (average + 0.9 * momentum_next)
    first_next = jnp.where(keep, first_state_value, adam_first_state[0])[None]
    second_next = jnp.where(keep, second_state_value, adam_second_state[0])[None]
    return (anchor_next, momentum_next, first_next, second_next)


def solution(mesh):
    in_specs = (
        P("rep", "fsdp", None),
        P("rep", "fsdp", None),
        P("rep", "fsdp"),
        P("rep", "fsdp", None),
        P("rep", "fsdp", None),
        P("rep", "fsdp", None),
        P("fsdp", None),
        P("fsdp", None),
    )
    out_specs = (P("fsdp", None), P("fsdp", None), P("rep", "fsdp", None), P("rep", "fsdp", None))
    return jax.shard_map(body, mesh=mesh, in_specs=in_specs, out_specs=out_specs, check_vma=False)
```

profile of v0, /device:TPU:6, one launch (start us, length us, event | category | flops | bytes accessed | tf_op | source)
XLA Modules:
  0.0 329.5 jit_solution(3314894536063248277)
XLA Ops:
  7.2 0.0 copy-start
  7.2 0.0 reduce-scatter.2.cloned.1.call-start
  7.2 1.8 copy-done
  9.1 5.5 %fusion = f32[3072,512]{1,0:T(8,128)} fusion(bf16[1,512,3072]{2,1,0:T(8,128)(2,1)S(1)} %copy-done, bf16[1,512,512]{2,1,0:T(8,128)(2,1)} %param.9), kind=kOutput, calls=%fused_computation | convolution fusion | flops 1610612736 | bytes 9961472 | tf_op jit(solution)/shard_map/dot_general | solution.py:24
  14.6 0.0 copy-start.5
  14.6 0.0 copy-start.1
  14.6 0.0 copy-start.2
  14.6 0.0 copy-start.3
  14.6 0.0 copy-start.4
  14.6 0.0 reduce-scatter.2.cloned.1.call-update
  14.6 0.0 all-reduce.2.cloned.1.call-start
  14.7 0.6 copy-done.5
  15.3 170.0 %reduce-scatter.2.cloned.1.call-done = f32[48,512]{1,0:T(8,128)} async-done(((f32[3072,512]{1,0:T(8,128)}), f32[48,512]{1,0:T(8,128)}) %reduce-scatter.2.cloned.1.call-update) | async-done | bytes 98320 | tf_op jit(solution)/shard_map/reduce_scatter | solution.py:23
  185.3 1.6 compare_reduce_fusion
  187.5 18.8 %pmax.7 = s32[]{:T(128)} all-reduce(s32[]{:T(128)S(6)} %convert_element_type.6), channel_id=1, replica_groups=mesh['rep'=12,'fsdp'=64] {'fsdp'}, use_global_device_ids=true, to_apply=%region_2.3 | all-reduce | flops 1 | bytes 8 | tf_op jit(solution)/shard_map/pmax | solution.py:40
  207.0 0.0 copy-done.1
  207.0 0.0 copy-done.2
  207.0 0.0 copy-done.3
  207.0 0.0 copy-done.4
  207.1 1.8 fusion.4
  208.8 0.0 all-reduce.2.cloned.1.call-update
  208.8 25.8 %psum.15 = f32[]{:T(128)} all-reduce(f32[]{:T(128)S(6)} %convert_element_type.7), channel_id=1, replica_groups=mesh['rep'=12,'fsdp'=64] {'rep'}, use_global_device_ids=true, to_apply=%region_4.5 | all-reduce | flops 1 | bytes 8 | tf_op jit(solution)/shard_map/psum | solution.py:43
  234.6 85.9 %all-reduce.2.cloned.1.call-done = f32[48,512]{1,0:T(8,128)} async-done(((f32[48,512]{1,0:T(8,128)}), f32[48,512]{1,0:T(8,128)}) %all-reduce.2.cloned.1.call-update) | async-done | bytes 98320 | tf_op jit(solution)/shard_map/psum | solution.py:43
  320.5 2.2 multiply_subtract_fusion
  (1 shorter events, 0.0 us)
Async XLA Ops:
  7.2 1.9 copy-start
  7.2 178.1 %reduce-scatter.2.cloned.1.call-start = ((), (), s32[]{:S(2)}) async-start(), calls=%async_computation.1 | async-start | bytes 6389760 | tf_op jit(solution)/shard_map/reduce_scatter | solution.py:23
  14.6 0.7 copy-start.5
  14.6 192.4 %copy-start.1 = (f32[48,512]{1,0:T(8,128)S(1)}, f32[48,512]{1,0:T(8,128)}, u32[]{:S(2)}) copy-start(f32[48,512]{1,0:T(8,128)} %param.14) | copy-start | bytes 294916
  14.6 192.4 %copy-start.2 = (f32[1,48,512]{2,1,0:T(8,128)S(1)}, f32[1,48,512]{2,1,0:T(8,128)}, u32[]{:S(2)}) copy-start(f32[1,48,512]{2,1,0:T(8,128)} %param.13) | copy-start | bytes 294916
  14.6 192.4 %copy-start.3 = (f32[1,48,512]{2,1,0:T(8,128)S(1)}, f32[1,48,512]{2,1,0:T(8,128)}, u32[]{:S(2)}) copy-start(f32[1,48,512]{2,1,0:T(8,128)} %param.12) | copy-start | bytes 294916
  14.6 192.4 %copy-start.4 = (f32[1,48,512]{2,1,0:T(8,128)S(1)}, f32[1,48,512]{2,1,0:T(8,128)}, u32[]{:S(2)}) copy-start(f32[1,48,512]{2,1,0:T(8,128)} %param.11) | copy-start | bytes 294916
  14.6 305.8 %all-reduce.2.cloned.1.call-start = ((), (), s32[]{:S(2)}) async-start(), calls=%async_computation.2 | async-start | bytes 196608 | tf_op jit(solution)/shard_map/psum | solution.py:43
Sparse Core Ops, SparseCore 0:
  14.8 170.4 reduce-scatter.1
  209.0 111.4 all-reduce.1
where the time goes:
time: 330 us
  waiting for transfers between devices  256 us (78%)
  blocking collectives  44.6 us (14%)
  between operations  15.4 us (5%)
  other arithmetic  5.58 us (2%)
  matrix products  5.54 us (2%)
    reduce_scatter x1, waiting for transfers between devices, body(): lax.psum_scatter(lax.dot_general(inputs, upstream, contract, preferred_el...  170 us
    psum x1, waiting for transfers between devices, body(): total, count = lax.psum((share, keep.astype(jnp.float32)), 'rep')  85.9 us
    psum x1, blocking collectives, body(): total, count = lax.psum((share, keep.astype(jnp.float32)), 'rep')  25.8 us
    pmax x1, blocking collectives, body(): replica_bad = lax.pmax(replica_nonfinite, 'fsdp')  18.8 us
  transfers between devices with their start and end apart: 2, of which 2 were waited for; matrix products, arithmetic and copies ran while one was open for 0% of the time, Pallas kernels for 0%

commit v1 on v0

v1 whole, which is shorter than its diff:
```python
import numpy as np
import jax
import jax.numpy as jnp
from jax import lax
from jax.sharding import Mesh, PartitionSpec as P

corr_first = 1.0 - 0.9**10
corr_second = 1.0 - 0.95**10

RS_MODE = "flat"
REP_MODE = "rsag"
FLAG_MODE = "global"


def fsdp_factors(mesh):
    row = mesh.devices[0]
    try:
        ys = sorted({d.coords[1] for d in row})
        xs = sorted({d.coords[0] for d in row})
        cs = sorted({d.core_on_chip for d in row})
        shape = (len(ys), len(xs), len(cs))
        if int(np.prod(shape)) != len(row):
            return None
        for i, d in enumerate(row):
            y, rest = divmod(i, shape[1] * shape[2])
            x, c = divmod(rest, shape[2])
            if (d.coords[1], d.coords[0], d.core_on_chip) != (ys[y], xs[x], cs[c]):
                return None
        return shape
    except (AttributeError, IndexError):
        return None


def solution(mesh):
    n_rep = mesh.shape["rep"]
    factors = fsdp_factors(mesh)
    if factors is None or RS_MODE == "flat":
        fine = Mesh(mesh.devices.reshape(n_rep, -1, 1, 1), ("rep", "y", "x", "core"))
    else:
        fine = Mesh(mesh.devices.reshape((n_rep,) + factors), ("rep", "y", "x", "core"))
    ny, nx, nc = fine.shape["y"], fine.shape["x"], fine.shape["core"]
    fsdp = ("y", "x", "core")

    def body(acts, cotangent, nonfinite_row_mask, params, adam_first_state, adam_second_state, anchor, momentum):
        rep = lax.axis_index("rep")
        marked = jnp.any(nonfinite_row_mask[0] == 1).astype(jnp.int32)
        if FLAG_MODE == "global":
            slots = (jnp.arange(n_rep) == rep).astype(jnp.int32) * marked
            bad_all = lax.psum(slots, ("rep",) + fsdp) > 0
            keep_all = jnp.logical_not(bad_all)
            keep = keep_all[rep]
            count = jnp.sum(keep_all.astype(jnp.float32))
        inputs = acts[0]
        upstream = cotangent[0]
        d = inputs.shape[1]
        rows = d // (ny * nx * nc)
        grouped = inputs.reshape(inputs.shape[0], ny, nx, nc, rows)
        partial = jnp.einsum("tyxcr,tk->cxyrk", grouped, upstream, preferred_element_type=jnp.float32)
        partial = partial.reshape(d, upstream.shape[1])
        if RS_MODE == "flat":
            gradient_value = lax.psum_scatter(partial, fsdp, scatter_dimension=0, tiled=True)
        elif RS_MODE == "staged":
            g = lax.psum_scatter(partial, "core", scatter_dimension=0, tiled=True)
            g = lax.psum_scatter(g, "x", scatter_dimension=0, tiled=True)
            gradient_value = lax.psum_scatter(g, "y", scatter_dimension=0, tiled=True)
        else:
            g = lax.psum_scatter(partial, "core", scatter_dimension=0, tiled=True)
            g = g.reshape(nx, -1, g.shape[-1])
            g = jnp.sum(lax.all_to_all(g, "x", 0, 0, tiled=True), axis=0)
            g = g.reshape(ny, -1, g.shape[-1])
            gradient_value = jnp.sum(lax.all_to_all(g, "y", 0, 0, tiled=True), axis=0)
        if FLAG_MODE != "global":
            has_nan = jnp.any(jnp.isnan(jnp.where((nonfinite_row_mask[0] == 1)[:, None], jnp.float32(jnp.nan), gradient_value)))
            keep = lax.pmax(has_nan.astype(jnp.int32), fsdp) == 0
            count = lax.psum(keep.astype(jnp.float32), "rep")
        corrupted_gradient = jnp.where((nonfinite_row_mask[0] == 1)[:, None], jnp.float32(jnp.nan), gradient_value)
        first_state_value = 0.9 * adam_first_state[0] + 0.1 * corrupted_gradient
        second_state_value = 0.95 * adam_second_state[0] + 0.05 * corrupted_gradient * corrupted_gradient
        update = first_state_value / corr_first / (jnp.sqrt(second_state_value / corr_second) + 1e-08)
        inner = params[0] - 0.1 * (update + 0.1 * params[0])
        pseudo = anchor - inner
        if REP_MODE == "psum":
            total = lax.psum(jnp.where(keep, pseudo, jnp.float32(0.0)), "rep")
        elif REP_MODE == "gather":
            every = lax.all_to_all(jnp.broadcast_to(pseudo, (n_rep,) + pseudo.shape), "rep", 0, 0, tiled=True)
            total = jnp.sum(jnp.where(keep_all[:, None, None], every, jnp.float32(0.0)), axis=0)
        else:
            share = jnp.where(keep, pseudo, jnp.float32(0.0))
            pieces = share.reshape(n_rep, -1, share.shape[-1]) if share.shape[0] % n_rep == 0 else None
            if pieces is None:
                total = lax.psum(share, "rep")
            else:
                mine = jnp.sum(lax.all_to_all(pieces, "rep", 0, 0, tiled=True), axis=0)
                total = lax.all_to_all(jnp.broadcast_to(mine, (n_rep,) + mine.shape), "rep", 0, 0, tiled=True)
                total = total.reshape(share.shape)
        average = total / count
        momentum_next = 0.9 * momentum + average
        anchor_next = anchor - 0.7 * (average + 0.9 * momentum_next)
        first_next = jnp.where(keep, first_state_value, adam_first_state[0])[None]
        second_next = jnp.where(keep, second_state_value, adam_second_state[0])[None]
        return (anchor_next, momentum_next, first_next, second_next)

    row3 = P("rep", ("y", "x", "core"), None)
    in_specs = (row3, row3, P("rep", ("y", "x", "core")), row3, row3, row3, P(("y", "x", "core"), None), P(("y", "x", "core"), None))
    out_specs = (P(("y", "x", "core"), None), P(("y", "x", "core"), None), row3, row3)
    return jax.shard_map(body, mesh=fine, in_specs=in_specs, out_specs=out_specs, check_vma=False)
```

time: 330 us -> 242 us (0.73)
  waiting for transfers between devices: 256 us -> 59.9 us
  blocking collectives: 44.6 us -> 141 us
  local copies, waits for them, and re-layouts: 2.42 us -> 12.9 us
  starting transfers between devices: 0.08 us -> 3.55 us
    reduce_scatter x1, waiting for transfers between devices: 170 us -> 48.9 us  [body(): lax.psum_scatter(partial, fsdp, scatter_dimension=0, tiled=True)]
    psum x1, blocking collectives: 25.8 us -> 119 us  [body(): bad_all = lax.psum(slots, ('rep',) + fsdp) > 0]
    psum x1 -> x0, waiting for transfers between devices: 85.9 us -> none  [body(): total, count = lax.psum((share, keep.astype(jnp.float32)), 'rep')]
    all_to_all x0 -> x1, blocking collectives: none -> 21.6 us  [body(): mine = jnp.sum(lax.all_to_all(pieces, 'rep', 0, 0, tiled=True), axis=0)]
    pmax x1 -> x0, blocking collectives: 18.8 us -> none  [body(): replica_bad = lax.pmax(replica_nonfinite, 'fsdp')]
    all_to_all x0 -> x1, waiting for transfers between devices: none -> 10.9 us  [body(): lax.all_to_all(jnp.broadcast_to(mine, (n_rep,) + mine.shape), 'rep', 0, 0...]
    transpose x0 -> x1, local copies, waits for them, and re-layouts: none -> 6.3 us  [body(): jnp.einsum('tyxcr,tk->cxyrk', grouped, upstream, preferred_element_type=j...]
    all_to_all x0 -> x1, starting transfers between devices: none -> 3.51 us  [body(): lax.all_to_all(jnp.broadcast_to(mine, (n_rep,) + mine.shape), 'rep', 0, 0...]
  transfers between devices with their start and end apart: 2 -> 2, of which waited for: 2 -> 2; matrix products, arithmetic and copies ran while one was open for 0% -> 1% of each run, Pallas kernels for 0% -> 0%
where the time goes in v1:
time: 242 us; the launch traced here: 241 us
  blocking collectives  141 us (58%)
  waiting for transfers between devices  59.9 us (25%)
  between operations  14.8 us (6%)
  local copies, waits for them, and re-layouts  12.9 us (5%)
  other arithmetic  5 us (2%)
  matrix products  4.41 us (2%)
  starting transfers between devices  3.55 us (1%)
    psum x1, blocking collectives, body(): bad_all = lax.psum(slots, ('rep',) + fsdp) > 0  119 us
    reduce_scatter x1, waiting for transfers between devices, body(): lax.psum_scatter(partial, fsdp, scatter_dimension=0, tiled=True)  48.9 us
    all_to_all x1, blocking collectives, body(): mine = jnp.sum(lax.all_to_all(pieces, 'rep', 0, 0, tiled=True), axis=0)  21.6 us
    all_to_all x1, waiting for transfers between devices, body(): lax.all_to_all(jnp.broadcast_to(mine, (n_rep,) + mine.shape), 'rep', 0, 0...  10.9 us
    transpose x1, local copies, waits for them, and re-layouts, body(): jnp.einsum('tyxcr,tk->cxyrk', grouped, upstream, preferred_element_type=j...  6.3 us
    unnamed x15, local copies, waits for them, and re-layouts  5.34 us
  transfers between devices with their start and end apart: 2, of which 2 were waited for; matrix products, arithmetic and copies ran while one was open for 1% of the time, Pallas kernels for 0%

profile of v1, /device:TPU:6, one launch (start us, length us, event | category | flops | bytes accessed | tf_op | source)
XLA Modules:
  0.0 241.3 jit_solution(13491523250778606136)
XLA Ops:
  7.2 0.0 copy-start
  7.2 0.0 reduce-scatter.2.cloned.1.call-start
  7.2 4.7 %copy.13 = bf16[1,512,3072]{1,2,0:T(8,128)(2,1)} copy(bf16[1,512,3072]{2,1,0:T(8,128)(2,1)} %param.8) | data formatting | bytes 6291456 | tf_op args[0]
  11.9 0.0 copy-done
  11.9 4.4 %fusion.2 = f32[1,1,64,48,512]{4,2,3,0,1:T(8,128)S(1)} fusion(bf16[512,64,48]{0,2,1:T(8,128)(2,1)} %bitcast.55, bf16[1,512,512]{2,1,0:T(8,128)(2,1)S(1)} %copy-done), kind=kOutput, calls=%fused_computation.2 | convolution fusion | flops 1610612736 | bytes 9961472 | tf_op jit(solution)/shard_map/tyxcr,tk->cxyrk/dot_general | solution.py:58
  16.4 6.3 %copy.15 = f32[1,1,64,48,512]{4,3,2,1,0:T(8,128)} copy(f32[1,1,64,48,512]{4,2,3,0,1:T(8,128)S(1)} %fusion.2) | data formatting | bytes 12582912 | tf_op jit(solution)/shard_map/tyxcr,tk->cxyrk/transpose | solution.py:58
  22.7 0.0 copy-start.6
  22.7 0.0 copy-start.1
  22.7 0.0 copy-start.2
  22.7 0.0 copy-start.3
  22.7 0.0 copy-start.4
  22.7 0.0 copy-start.5
  22.7 0.0 reduce-scatter.2.cloned.1.call-update
  22.7 0.6 copy-done.6
  23.3 0.6 compare_reduce_fusion
  24.6 119.1 %psum.7 = s32[12]{0:T(128)S(1)} all-reduce(s32[12]{0:T(128)S(1)} %compare_select_fusion), channel_id=1, replica_groups=mesh['rep'=12,'fsdp'=64] {'rep','fsdp'}, use_global_device_ids=true, to_apply=%region_1.0 | all-reduce | flops 12 | bytes 96 | tf_op jit(solution)/shard_map/psum | solution.py:49
  143.8 0.6 dynamic_slice.3
  144.4 48.9 %reduce-scatter.2.cloned.1.call-done = f32[48,512]{1,0:T(8,128)} async-done(((f32[3072,512]{1,0:T(8,128)}), f32[48,512]{1,0:T(8,128)}) %reduce-scatter.2.cloned.1.call-update) | async-done | bytes 98320 | tf_op jit(solution)/shard_map/reduce_scatter | solution.py:61
  193.3 0.0 copy-done.1
  193.3 0.0 copy-done.2
  193.3 0.0 copy-done.3
  193.3 0.0 copy-done.4
  193.3 2.4 fusion.7
  195.7 21.6 %all_to_all.10 = f32[12,4,512]{2,1,0:T(4,128)S(1)} all-to-all(f32[12,4,512]{2,1,0:T(4,128)S(1)} %reshape.31), channel_id=1, replica_groups=mesh['rep'=12,'fsdp'=64] {'rep'}, dimensions={0} | all-to-all | bytes 196608 | tf_op jit(solution)/shard_map/all_to_all | solution.py:93
  217.3 0.7 broadcast_in_dim.29
  217.9 3.5 %all-to-all-start.1 = ((f32[12,4,512]{2,1,0:T(4,128)}), f32[12,4,512]{2,1,0:T(4,128)S(1)}, u32[]{:S(2)}, u32[]{:S(2)}) async-start(f32[12,4,512]{2,1,0:T(4,128)} %broadcast_in_dim.29), calls=%async_computation.2 | async-start | bytes 196608 | tf_op jit(solution)/shard_map/all_to_all | solution.py:94
  221.5 0.6 convert_reduce_fusion
  222.1 10.9 %all-to-all-done.1 = f32[12,4,512]{2,1,0:T(4,128)S(1)} async-done(((f32[12,4,512]{2,1,0:T(4,128)}), f32[12,4,512]{2,1,0:T(4,128)S(1)}, u32[]{:S(2)}, u32[]{:S(2)}) %all-to-all-start.1) | async-done | bytes 98336 | tf_op jit(solution)/shard_map/all_to_all | solution.py:94
  233.0 0.7 broadcast_divide_fusion
  233.7 0.0 copy-done.5
  233.7 0.7 multiply_subtract_fusion
  (5 shorter events, 0.1 us)
Async XLA Ops:
  7.2 4.8 %copy-start = (bf16[1,512,512]{2,1,0:T(8,128)(2,1)S(1)}, bf16[1,512,512]{2,1,0:T(8,128)(2,1)}, u32[]{:S(2)}) copy-start(bf16[1,512,512]{2,1,0:T(8,128)(2,1)} %param.9) | copy-start | bytes 1572868
  7.2 186.1 %reduce-scatter.2.cloned.1.call-start = ((), (), s32[]{:S(2)}) async-start(), calls=%async_computation.3 | async-start | bytes 6389760 | tf_op jit(solution)/shard_map/reduce_scatter | solution.py:61
  22.7 0.7 copy-start.6
  22.7 170.6 %copy-start.1 = (f32[48,512]{1,0:T(8,128)S(1)}, f32[48,512]{1,0:T(8,128)}, u32[]{:S(2)}) copy-start(f32[48,512]{1,0:T(8,128)} %param.14) | copy-start | bytes 294916
  22.7 170.6 %copy-start.2 = (f32[1,48,512]{2,1,0:T(8,128)S(1)}, f32[1,48,512]{2,1,0:T(8,128)}, u32[]{:S(2)}) copy-start(f32[1,48,512]{2,1,0:T(8,128)} %param.13) | copy-start | bytes 294916
  22.7 170.6 %copy-start.3 = (f32[1,48,512]{2,1,0:T(8,128)S(1)}, f32[1,48,512]{2,1,0:T(8,128)}, u32[]{:S(2)}) copy-start(f32[1,48,512]{2,1,0:T(8,128)} %param.12) | copy-start | bytes 294916
  22.7 170.6 %copy-start.4 = (f32[1,48,512]{2,1,0:T(8,128)S(1)}, f32[1,48,512]{2,1,0:T(8,128)}, u32[]{:S(2)}) copy-start(f32[1,48,512]{2,1,0:T(8,128)} %param.11) | copy-start | bytes 294916
  22.7 211.0 %copy-start.5 = (f32[48,512]{1,0:T(8,128)S(1)}, f32[48,512]{1,0:T(8,128)}, u32[]{:S(2)}) copy-start(f32[48,512]{1,0:T(8,128)} %param.15) | copy-start | bytes 294916
  217.9 15.0 %all-to-all-start.1 = ((f32[12,4,512]{2,1,0:T(4,128)}), f32[12,4,512]{2,1,0:T(4,128)S(1)}, u32[]{:S(2)}, u32[]{:S(2)}) async-start(f32[12,4,512]{2,1,0:T(4,128)} %broadcast_in_dim.29), calls=%async_computation.2 | async-start | bytes 196608 | tf_op jit(solution)/shard_map/all_to_all | solution.py:94
Sparse Core Ops, SparseCore 0:
  22.8 170.3 reduce-scatter.1

commit v2 on v1

--- a/solution.py
+++ b/solution.py
@@ -54,9 +54,13 @@
         upstream = cotangent[0]
         d = inputs.shape[1]
         rows = d // (ny * nx * nc)
-        grouped = inputs.reshape(inputs.shape[0], ny, nx, nc, rows)
-        partial = jnp.einsum("tyxcr,tk->cxyrk", grouped, upstream, preferred_element_type=jnp.float32)
-        partial = partial.reshape(d, upstream.shape[1])
+        if RS_MODE == "flat":
+            contract = (((0,), (0,)), ((), ()))
+            partial = lax.dot_general(inputs, upstream, contract, preferred_element_type=jnp.float32)
+        else:
+            grouped = inputs.reshape(inputs.shape[0], ny, nx, nc, rows)
+            partial = jnp.einsum("tyxcr,tk->cxyrk", grouped, upstream, preferred_element_type=jnp.float32)
+            partial = partial.reshape(d, upstream.shape[1])
         if RS_MODE == "flat":
             gradient_value = lax.psum_scatter(partial, fsdp, scatter_dimension=0, tiled=True)
         elif RS_MODE == "staged":

time: 242 us -> 235 us (0.971)
  local copies, waits for them, and re-layouts: 12.9 us -> 3.78 us
    transpose x1 -> x0, local copies, waits for them, and re-layouts: 6.3 us -> none  [body(): jnp.einsum('tyxcr,tk->cxyrk', grouped, upstream, preferred_element_type=j...]
    unnamed x15 -> x10, local copies, waits for them, and re-layouts: 5.34 us -> 2.47 us
where the time goes in v2:
time: 235 us; the launch traced here: 234 us
  blocking collectives  141 us (60%)
  waiting for transfers between devices  59.8 us (25%)
  between operations  14.7 us (6%)
  other arithmetic  5.94 us (3%)
  matrix products  5.54 us (2%)
  local copies, waits for them, and re-layouts  3.78 us (2%)
  starting transfers between devices  3.55 us (2%)
    psum x1, blocking collectives, body(): bad_all = lax.psum(slots, ('rep',) + fsdp) > 0  119 us
    reduce_scatter x1, waiting for transfers between devices, body(): lax.psum_scatter(partial, fsdp, scatter_dimension=0, tiled=True)  48.9 us
    all_to_all x1, blocking collectives, body(): mine = jnp.sum(lax.all_to_all(pieces, 'rep', 0, 0, tiled=True), axis=0)  21.5 us
    all_to_all x1, waiting for transfers between devices, body(): lax.all_to_all(jnp.broadcast_to(mine, (n_rep,) + mine.shape), 'rep', 0, 0...  10.9 us
    dot_general x1, matrix products, body(): lax.dot_general(inputs, upstream, contract, preferred_element_type=jnp.fl...  5.54 us
  transfers between devices with their start and end apart: 2, of which 2 were waited for; matrix products, arithmetic and copies ran while one was open for 1% of the time, Pallas kernels for 0%

profile of v2, /device:TPU:6, one launch (start us, length us, event | category | flops | bytes accessed | tf_op | source)
XLA Modules:
  0.0 234.0 jit_solution(408256258489669289)
XLA Ops:
  7.2 0.0 copy-start
  7.2 0.0 reduce-scatter.2.cloned.1.call-start
  7.2 1.8 copy-done
  9.1 5.5 %fusion = f32[3072,512]{1,0:T(8,128)} fusion(bf16[1,512,3072]{2,1,0:T(8,128)(2,1)S(1)} %copy-done, bf16[1,512,512]{2,1,0:T(8,128)(2,1)} %param.9), kind=kOutput, calls=%fused_computation | convolution fusion | flops 1610612736 | bytes 9961472 | tf_op jit(solution)/shard_map/dot_general | solution.py:59
  14.6 0.0 copy-start.4
  14.6 0.0 copy-start.1
  14.6 0.0 copy-start.2
  14.6 0.0 copy-start.3
  14.6 0.0 reduce-scatter.2.cloned.1.call-update
  14.6 0.6 copy-done.4
  15.3 0.6 compare_reduce_fusion
  16.6 119.0 %psum.7 = s32[12]{0:T(128)S(1)} all-reduce(s32[12]{0:T(128)S(1)} %compare_select_fusion), channel_id=1, replica_groups=mesh['rep'=12,'fsdp'=64] {'rep','fsdp'}, use_global_device_ids=true, to_apply=%region_1.0 | all-reduce | flops 12 | bytes 96 | tf_op jit(solution)/shard_map/psum | solution.py:49
  135.6 0.6 dynamic_slice.3
  136.2 48.9 %reduce-scatter.2.cloned.1.call-done = f32[48,512]{1,0:T(8,128)} async-done(((f32[3072,512]{1,0:T(8,128)}), f32[48,512]{1,0:T(8,128)}) %reduce-scatter.2.cloned.1.call-update) | async-done | bytes 98320 | tf_op jit(solution)/shard_map/reduce_scatter | solution.py:65
  185.1 0.0 copy-done.1
  185.1 0.0 copy-done.2
  185.1 0.0 copy-done.3
  185.1 2.4 %fusion.4 = (f32[1,48,512]{2,1,0:T(8,128)}, f32[48,512]{1,0:T(8,128)S(1)}, f32[1,48,512]{2,1,0:T(8,128)}) fusion(f32[1,48,512]{2,1,0:T(8,128)S(1)} %copy-done.2, f32[48,512]{1,0:T(8,128)} %reduce-scatter.2.cloned.1.call-done, pred[48]{0:T(512)(128)(4,1)S(1)} %get-tuple-element.10, pred[]{:T(512)} %bitcast, f32[48,512]{1,0:T(8,128)S(1)} %copy-done.1, ...), kind=kLoop, calls=%fused_computation.7 | loop fusion | flops 491520 | bytes 786481 | tf_op jit(solution)/shard_map/broadcast_in_dim | solution.py:104
  187.5 21.5 %all_to_all.10 = f32[12,4,512]{2,1,0:T(4,128)S(1)} all-to-all(f32[12,4,512]{2,1,0:T(4,128)S(1)} %reshape.21), channel_id=1, replica_groups=mesh['rep'=12,'fsdp'=64] {'rep'}, dimensions={0} | all-to-all | bytes 196608 | tf_op jit(solution)/shard_map/all_to_all | solution.py:97
  209.1 0.7 broadcast_in_dim.29
  209.8 3.5 %all-to-all-start.1 = ((f32[12,4,512]{2,1,0:T(4,128)}), f32[12,4,512]{2,1,0:T(4,128)S(1)}, u32[]{:S(2)}, u32[]{:S(2)}) async-start(f32[12,4,512]{2,1,0:T(4,128)} %broadcast_in_dim.29), calls=%async_computation.2 | async-start | bytes 196608 | tf_op jit(solution)/shard_map/all_to_all | solution.py:98
  213.3 0.6 convert_reduce_fusion
  213.9 10.9 %all-to-all-done.1 = f32[12,4,512]{2,1,0:T(4,128)S(1)} async-done(((f32[12,4,512]{2,1,0:T(4,128)}), f32[12,4,512]{2,1,0:T(4,128)S(1)}, u32[]{:S(2)}, u32[]{:S(2)}) %all-to-all-start.1) | async-done | bytes 98336 | tf_op jit(solution)/shard_map/all_to_all | solution.py:98
  224.8 0.7 broadcast_divide_fusion
  225.5 1.6 multiply_subtract_fusion
  (5 shorter events, 0.1 us)
Async XLA Ops:
  7.2 1.9 copy-start
  7.2 177.9 %reduce-scatter.2.cloned.1.call-start = ((), (), s32[]{:S(2)}) async-start(), calls=%async_computation.3 | async-start | bytes 6389760 | tf_op jit(solution)/shard_map/reduce_scatter | solution.py:65
  14.6 0.7 copy-start.4
  14.6 170.5 %copy-start.1 = (f32[48,512]{1,0:T(8,128)S(1)}, f32[48,512]{1,0:T(8,128)}, u32[]{:S(2)}) copy-start(f32[48,512]{1,0:T(8,128)} %param.14) | copy-start | bytes 294916
  14.6 170.5 %copy-start.2 = (f32[1,48,512]{2,1,0:T(8,128)S(1)}, f32[1,48,512]{2,1,0:T(8,128)}, u32[]{:S(2)}) copy-start(f32[1,48,512]{2,1,0:T(8,128)} %param.13) | copy-start | bytes 294916
  14.6 170.5 %copy-start.3 = (f32[1,48,512]{2,1,0:T(8,128)S(1)}, f32[1,48,512]{2,1,0:T(8,128)}, u32[]{:S(2)}) copy-start(f32[1,48,512]{2,1,0:T(8,128)} %param.12) | copy-start | bytes 294916
  209.8 15.0 %all-to-all-start.1 = ((f32[12,4,512]{2,1,0:T(4,128)}), f32[12,4,512]{2,1,0:T(4,128)S(1)}, u32[]{:S(2)}, u32[]{:S(2)}) async-start(f32[12,4,512]{2,1,0:T(4,128)} %broadcast_in_dim.29), calls=%async_computation.2 | async-start | bytes 196608 | tf_op jit(solution)/shard_map/all_to_all | solution.py:98
Sparse Core Ops, SparseCore 0:
  14.8 170.2 reduce-scatter.1
